TPU v7x, 128 devices: a whole 4x4x4 slice. The times are simulated.
128 devices in a mesh: tile: 16 (over z_hi, x, core), lag: 8 (over z_lo, y).
Axes of the slice: x: 4, y: 4, z: 4 (z_hi: 2, z_lo: 2; z = z_hi * 2 + z_lo), core: 2. Of those that a mesh axis runs over, the one named last changes fastest.
Arguments:
- history: bfloat16 [16, 128, 384, 512], P('lag', 'tile'), may hold values from -6 to 6
- lag_blocks: bfloat16 [16, 128, 2, 384, 384], P('lag', 'tile'), may hold values from -0.0625 to 0.0625
- self_inverse: bfloat16 [128, 384, 384], P('tile'), may hold values from -0.3125 to 0.3125
- excitation: float32 [128, 384, 512], P('tile'), may hold values from -6 to 6
- pattern: int32 [16, 128, 2], P('lag', 'tile'), may hold values from 0 to 8
- live_counts: int32 [16, 128], P('lag', 'tile'), may hold values from 1 to 2
Outputs:
- traction: bfloat16 [128, 384, 512], P('tile')
- shifted_history: bfloat16 [16, 128, 384, 512], P('lag', 'tile')
All inputs are finite; a program needn't handle non-finite values.
Results may differ from a plain program's by a relative error of at most 0.013.
Values may be sent and summed in bfloat16 or wider, within the bound.
No kernel may reach another device: no remote copies, remote signals or barrier semaphores. Data moves between devices by JAX's collectives and lax.ppermute only.
A program may use at most 128 MiB of HBM per device.

v0:
```python
import jax
import jax.numpy as jnp
from jax import lax
from jax.sharding import PartitionSpec as P

SLOTS = 2
EDGE = 4


def padded(cells, sides, width):
    for axis, dim in sides:
        count = lax.axis_size(axis)
        head = lax.slice_in_dim(cells, 0, width, axis=dim)
        tail = lax.slice_in_dim(cells, cells.shape[dim] - width, cells.shape[dim], axis=dim)
        cells = jnp.concatenate(
            [
                lax.ppermute(tail, axis, [(i, (i + 1) % count) for i in range(count)]),
                cells,
                lax.ppermute(head, axis, [((i + 1) % count, i) for i in range(count)]),
            ],
            axis=dim,
        )
    return cells


def passed_along(array, axis, by):
    length = lax.axis_size(axis)
    pairs = [(i, i + by) for i in range(length) if 0 <= i + by < length]
    return lax.ppermute(array, axis, pairs)


def pick_sources(window, source_index):
    return window[source_index]


def shards(history, lag_blocks, self_inverse, excitation, pattern, live_counts):
    blocks_here = history.shape[1]
    window = padded(history, (("tile", 1),), EDGE)
    positions = jnp.arange(blocks_here, dtype=jnp.int32)
    source_index = positions[None, :, None] + pattern
    sources = jax.vmap(pick_sources)(window, source_index)
    live = jnp.arange(SLOTS, dtype=jnp.int32)[None, None, :] < live_counts[:, :, None]
    sources = sources * live[:, :, :, None, None].astype(sources.dtype)
    partial_field = jnp.einsum(
        "lbsij,lbsjr->bir", lag_blocks, sources, preferred_element_type=jnp.float32
    )
    carried = passed_along(history[-1], "lag", 1)
    field = lax.psum(partial_field.astype(jnp.bfloat16), "lag").astype(jnp.float32)
    residual = (excitation - field).astype(jnp.bfloat16)
    traction = jnp.einsum(
        "bij,bjr->bir", self_inverse, residual, preferred_element_type=jnp.float32
    ).astype(jnp.bfloat16)
    newest = jnp.where(lax.axis_index("lag") == 0, traction, carried)
    shifted_history = jnp.concatenate([newest[None], history[:-1]], axis=0)
    return (traction, shifted_history)


def solution(mesh):
    in_specs = (
        P("lag", "tile", None, None),
        P("lag", "tile", None, None, None),
        P("tile", None, None),
        P("tile", None, None),
        P("lag", "tile", None),
        P("lag", "tile"),
    )
    out_specs = (P("tile", None, None), P("lag", "tile", None, None))
    return jax.shard_map(shards, mesh=mesh, in_specs=in_specs, out_specs=out_specs, check_vma=False)
```

profile of v0, /device:TPU:33, one launch (start us, length us, event | category | flops | bytes accessed | tf_op | source)
XLA Modules:
  0.0 263.7 jit_solution(10920987208944018283)
XLA Ops:
  7.2 0.0 copy-start
  7.2 0.0 copy-start.2
  7.2 0.0 copy-start.3
  7.2 0.0 all-reduce.2.cloned.1.call-start
  7.2 6.2 %fusion.13 = (bf16[2,4,384,512]{3,2,1,0:T(8,128)(2,1)}, bf16[2,4,384,512]{3,2,1,0:T(8,128)(2,1)}) fusion(bf16[2,8,384,512]{3,2,1,0:T(8,128)(2,1)} %param.6), kind=kLoop, calls=%fused_computation.20 | loop fusion | bytes 12582912 | tf_op jit(solution)/shard_map/slice | solution.py:14
  13.5 1.8 collective-permute-start
  15.3 0.0 collective-permute-start.1
  15.3 0.0 copy-done.2
  15.3 0.1 copy.14
  15.4 0.1 reshape.10
  15.5 0.0 copy-done.3
  15.5 0.1 fusion.7
  15.5 34.2 %collective-permute-done = bf16[2,4,384,512]{3,2,1,0:T(8,128)(2,1)} collective-permute-done((bf16[2,4,384,512]{3,2,1,0:T(8,128)(2,1)}, bf16[2,4,384,512]{3,2,1,0:T(8,128)(2,1)}, u32[]{:S(2)}, u32[]{:S(2)}) %collective-permute-start) | collective-permute-done | bytes 3145760 | tf_op jit(solution)/shard_map/ppermute | solution.py:17
  49.8 2.8 %collective-permute-done.1 = bf16[2,4,384,512]{3,2,1,0:T(8,128)(2,1)} collective-permute-done((bf16[2,4,384,512]{3,2,1,0:T(8,128)(2,1)}, bf16[2,4,384,512]{3,2,1,0:T(8,128)(2,1)}, u32[]{:S(2)}, u32[]{:S(2)}) %collective-permute-start.1) | collective-permute-done | bytes 3145760 | tf_op jit(solution)/shard_map/ppermute | solution.py:19
  52.6 10.5 %pad_maximum_fusion = bf16[2,16,384,512]{3,2,1,0:T(8,128)(2,1)} fusion(bf16[2,4,384,512]{3,2,1,0:T(8,128)(2,1)} %collective-permute-done.1, bf16[2,8,384,512]{3,2,1,0:T(8,128)(2,1)} %param.6, bf16[2,4,384,512]{3,2,1,0:T(8,128)(2,1)} %collective-permute-done), kind=kLoop, calls=%fused_computation.1 | loop fusion | flops 12582912 | bytes 25165824 | tf_op jit(solution)/shard_map/concatenate | solution.py:15
  63.1 11.4 %gather_fusion = bf16[32,384,512]{2,1,0:T(8,128)(2,1)} fusion(bf16[2,16,384,512]{3,2,1,0:T(8,128)(2,1)} %pad_maximum_fusion, s32[32]{0:T(128)S(1)} %reshape.10), kind=kCustom, calls=%fused_computation | custom fusion | bytes 25166080 | tf_op jit(solution)/shard_map/vmap()/gather | solution.py:33
  74.5 12.6 %fusion.4 = bf16[8,384,512]{2,1,0:T(8,128)(2,1)} fusion(bf16[2,8,2,384,384]{4,3,2,1,0:T(8,128)(2,1)} %param.7, bf16[2,8,2,384,512]{4,3,2,1,0:T(8,128)(2,1)} %bitcast.24, bf16[2,8,2]{2,1,0:T(8,128)(2,1)S(1)} %fusion.7), kind=kOutput, calls=%fused_computation.9 | convolution fusion | flops 4858576896 | bytes 25165888 | tf_op jit(solution)/shard_map/lbsij,lbsjr->bir/dot_general | solution.py:44
  87.1 0.0 all-reduce.2.cloned.1.call-update
  87.1 6.1 %fusion.12 = (bf16[1,8,384,512]{3,2,1,0:T(8,128)(2,1)}, bf16[1,8,384,512]{3,2,1,0:T(8,128)(2,1)}) fusion(bf16[2,8,384,512]{3,2,1,0:T(8,128)(2,1)} %param.6), kind=kLoop, calls=%fused_computation.19 | loop fusion | bytes 12582912 | tf_op jit(solution)/shard_map/slice | solution.py:47
  93.2 4.7 %copy.22 = bf16[1,8,384,512]{2,3,1,0:T(8,128)(2,1)} copy(bf16[1,8,384,512]{3,2,1,0:T(8,128)(2,1)} %get-tuple-element.6) | data formatting | bytes 6291456
  97.9 3.2 %collective-permute-start.2 = (bf16[8,384,512]{1,2,0:T(8,128)(2,1)}, bf16[8,384,512]{1,2,0:T(8,128)(2,1)}, u32[]{:S(2)}, u32[]{:S(2)}) collective-permute-start(bf16[8,384,512]{1,2,0:T(8,128)(2,1)} %bitcast.25), channel_id=1, source_target_pairs={{0,1},{1,2},{2,3},{3,4},{4,5},{5,6},{6,7},{8,9},{9,10},{10,11},{11... | collective-permute-start | bytes 9437192 | tf_op jit(solution)/shard_map/ppermute | solution.py:29
  101.2 4.6 %copy.23 = bf16[1,8,384,512]{2,3,1,0:T(8,128)(2,1)} copy(bf16[1,8,384,512]{3,2,1,0:T(8,128)(2,1)} %get-tuple-element.7) | data formatting | bytes 6291456
  105.8 124.0 %all-reduce.2.cloned.1.call-done = bf16[8,384,512]{2,1,0:T(8,128)(2,1)} async-done(((bf16[8,384,512]{2,1,0:T(8,128)(2,1)}), bf16[8,384,512]{2,1,0:T(8,128)(2,1)}) %all-reduce.2.cloned.1.call-update) | async-done | bytes 3145744 | tf_op jit(solution)/shard_map/psum | solution.py:48
  229.8 0.0 copy-done
  229.8 7.6 %convert_bitcast_fusion = bf16[8,384,512]{1,2,0:T(8,128)(2,1)} fusion(bf16[8,384,384]{2,1,0:T(8,128)(2,1)S(1)} %copy-done, f32[8,384,512]{2,1,0:T(8,128)} %param.9, bf16[8,384,512]{2,1,0:T(8,128)(2,1)} %all-reduce.2.cloned.1.call-done), kind=kOutput, calls=%fused_computation.11 | convolution fusion | flops 1214251008 | bytes 14942208 | tf_op jit(solution)/shard_map/bij,bjr->bir/dot_general | solution.py:50
  237.4 4.6 %copy.18 = bf16[8,384,512]{2,1,0:T(8,128)(2,1)} copy(bf16[8,384,512]{1,2,0:T(8,128)(2,1)} %convert_bitcast_fusion) | data formatting | bytes 6291456
  242.0 0.0 copy-start.1
  242.0 0.0 collective-permute-done.2
  242.0 2.4 select_bitcast_fusion
  244.4 0.4 copy-done.1
  244.9 3.4 %pad_maximum_fusion.1 = bf16[2,8,384,512]{2,3,1,0:T(8,128)(2,1)} fusion(bf16[1,8,384,512]{2,3,1,0:T(8,128)(2,1)S(1)} %copy-done.1, bf16[1,8,384,512]{2,3,1,0:T(8,128)(2,1)S(1)} %select_bitcast_fusion), kind=kLoop, calls=%fused_computation.4 | loop fusion | flops 3145728 | bytes 12582912 | tf_op jit(solution)/shard_map/concatenate | solution.py:54
  248.2 8.6 %copy.19 = bf16[2,8,384,512]{3,2,1,0:T(8,128)(2,1)} copy(bf16[2,8,384,512]{2,3,1,0:T(8,128)(2,1)} %pad_maximum_fusion.1) | data formatting | bytes 12582912
  (1 shorter events, 0.0 us)
Async XLA Ops:
  7.2 222.6 %copy-start = (bf16[8,384,384]{2,1,0:T(8,128)(2,1)S(1)}, bf16[8,384,384]{2,1,0:T(8,128)(2,1)}, u32[]{:S(2)}) copy-start(bf16[8,384,384]{2,1,0:T(8,128)(2,1)} %param.8) | copy-start | bytes 7077892
  7.2 8.1 %copy-start.2 = (s32[2,8,2]{1,2,0:T(2,128)S(1)}, s32[2,8,2]{1,2,0:T(2,128)}, u32[]{:S(2)}) copy-start(s32[2,8,2]{1,2,0:T(2,128)} %param.10) | copy-start | bytes 388
  7.2 8.3 %copy-start.3 = (s32[2,8]{1,0:T(2,128)S(1)}, s32[2,8]{1,0:T(2,128)}, u32[]{:S(2)}) copy-start(s32[2,8]{1,0:T(2,128)} %param.11) | copy-start | bytes 196
  7.2 222.6 %all-reduce.2.cloned.1.call-start = ((), (), s32[]{:S(2)}) async-start(), calls=%async_computation | async-start | bytes 6291456 | tf_op jit(solution)/shard_map/psum | solution.py:48
  13.5 36.3 %collective-permute-start = (bf16[2,4,384,512]{3,2,1,0:T(8,128)(2,1)}, bf16[2,4,384,512]{3,2,1,0:T(8,128)(2,1)}, u32[]{:S(2)}, u32[]{:S(2)}) collective-permute-start(bf16[2,4,384,512]{3,2,1,0:T(8,128)(2,1)} %get-tuple-element.8), channel_id=1, source_target_pairs={{0,8},{8,16},{16,24},{24,32},{32,40},{40,48},{48,56},{56,64},{64,7... | collective-permute-start | bytes 9437192 | tf_op jit(solution)/shard_map/ppermute | solution.py:17
  15.3 37.3 %collective-permute-start.1 = (bf16[2,4,384,512]{3,2,1,0:T(8,128)(2,1)}, bf16[2,4,384,512]{3,2,1,0:T(8,128)(2,1)}, u32[]{:S(2)}, u32[]{:S(2)}) collective-permute-start(bf16[2,4,384,512]{3,2,1,0:T(8,128)(2,1)} %get-tuple-element.9), channel_id=1, source_target_pairs={{8,0},{16,8},{24,16},{32,24},{40,32},{48,40},{56,48},{64,56},{72,6... | collective-permute-start | bytes 9437192 | tf_op jit(solution)/shard_map/ppermute | solution.py:19
  97.9 144.1 %collective-permute-start.2 = (bf16[8,384,512]{1,2,0:T(8,128)(2,1)}, bf16[8,384,512]{1,2,0:T(8,128)(2,1)}, u32[]{:S(2)}, u32[]{:S(2)}) collective-permute-start(bf16[8,384,512]{1,2,0:T(8,128)(2,1)} %bitcast.25), channel_id=1, source_target_pairs={{0,1},{1,2},{2,3},{3,4},{4,5},{5,6},{6,7},{8,9},{9,10},{10,11},{11... | collective-permute-start | bytes 9437192 | tf_op jit(solution)/shard_map/ppermute | solution.py:29
  242.0 2.8 %copy-start.1 = (bf16[1,8,384,512]{2,3,1,0:T(8,128)(2,1)S(1)}, bf16[1,8,384,512]{2,3,1,0:T(8,128)(2,1)}, u32[]{:S(2)}) copy-start(bf16[1,8,384,512]{2,3,1,0:T(8,128)(2,1)} %copy.23) | copy-start | bytes 9437188
Sparse Core Ops, SparseCore 0:
  87.3 142.4 all-reduce.1
where the time goes:
time: 264 us
  waiting for transfers between devices  161 us (61%)
  local copies, waits for them, and re-layouts  47 us (18%)
  matrix products  20.2 us (8%)
  other arithmetic  16.4 us (6%)
  between operations  14.1 us (5%)
  starting transfers between devices  5.01 us (2%)
    psum x1, waiting for transfers between devices, shards(): lax.psum(partial_field.astype(jnp.bfloat16), 'lag').astype(jnp.float32)  124 us
    ppermute x1, waiting for transfers between devices, padded(): lax.ppermute(tail, axis, [(i, (i + 1) % count) for i in range(count)])  34.2 us
    unnamed x12, local copies, waits for them, and re-layouts  23.1 us
    dot_general x1, matrix products, shards(): jnp.einsum('lbsij,lbsjr->bir', lag_blocks, sources, preferred_element_typ...  12.6 us
    gather x3, local copies, waits for them, and re-layouts, pick_sources(): return window[source_index]  11.6 us
    concatenate x1, other arithmetic, padded(): jnp.concatenate([lax.ppermute(tail, axis, [(i, (i + 1) % count) for i in...  10.5 us
    dot_general x1, matrix products, shards(): jnp.einsum('bij,bjr->bir', self_inverse, residual, preferred_element_type...  7.62 us
    slice x1, local copies, waits for them, and re-layouts, padded(): lax.slice_in_dim(cells, cells.shape[dim] - width, cells.shape[dim], axis=...  6.25 us
  transfers between devices with their start and end apart: 4, of which 3 were waited for; matrix products, arithmetic and copies ran while one was open for 11% of the time, Pallas kernels for 0%

commit v1 on v0

--- a/solution.py
+++ b/solution.py
@@ -45,7 +45,9 @@
         "lbsij,lbsjr->bir", lag_blocks, sources, preferred_element_type=jnp.float32
     )
     carried = passed_along(history[-1], "lag", 1)
-    field = lax.psum(partial_field.astype(jnp.bfloat16), "lag").astype(jnp.float32)
+    field = jnp.sum(lax.all_gather(partial_field.astype(jnp.bfloat16), "lag"), axis=0).astype(
+        jnp.float32
+    )
     residual = (excitation - field).astype(jnp.bfloat16)
     traction = jnp.einsum(
         "bij,bjr->bir", self_inverse, residual, preferred_element_type=jnp.float32

time: 264 us -> 484 us (1.83)
  waiting for transfers between devices: 161 us -> 331 us
  local copies, waits for them, and re-layouts: 47 us -> 79.7 us
  other arithmetic: 16.4 us -> 31.6 us
    all_gather x0 -> x1, waiting for transfers between devices: none -> 294 us  [shards(): lax.all_gather(partial_field.astype(jnp.bfloat16), 'lag')]
    psum x1 -> x0, waiting for transfers between devices: 124 us -> none  [shards(): lax.psum(partial_field.astype(jnp.bfloat16), 'lag').astype(jnp.float32)]
    gather x3 -> x4, local copies, waits for them, and re-layouts: 11.6 us -> 28.2 us  [pick_sources(): return window[source_index]]
    reduce_sum x0 -> x1, other arithmetic: none -> 15.3 us  [shards(): jnp.sum(lax.all_gather(partial_field.astype(jnp.bfloat16), 'lag'), axis=0)]
    unnamed x12 -> x14, local copies, waits for them, and re-layouts: 23.1 us -> 34.4 us
where the time goes in v1:
time: 484 us; the launch traced here: 483 us
  waiting for transfers between devices  331 us (68%)
  local copies, waits for them, and re-layouts  79.7 us (16%)
  other arithmetic  31.6 us (7%)
  matrix products  21.1 us (4%)
  between operations  14.1 us (3%)
  starting transfers between devices  5.19 us (1%)
    all_gather x1, waiting for transfers between devices, shards(): lax.all_gather(partial_field.astype(jnp.bfloat16), 'lag')  294 us
    unnamed x14, local copies, waits for them, and re-layouts  34.4 us
    ppermute x1, waiting for transfers between devices, padded(): lax.ppermute(tail, axis, [(i, (i + 1) % count) for i in range(count)])  34.2 us
    gather x4, local copies, waits for them, and re-layouts, pick_sources(): return window[source_index]  28.2 us
    reduce_sum x1, other arithmetic, shards(): jnp.sum(lax.all_gather(partial_field.astype(jnp.bfloat16), 'lag'), axis=0)  15.3 us
    dot_general x1, matrix products, shards(): jnp.einsum('lbsij,lbsjr->bir', lag_blocks, sources, preferred_element_typ...  13.6 us
    concatenate x1, other arithmetic, padded(): jnp.concatenate([lax.ppermute(tail, axis, [(i, (i + 1) % count) for i in...  10.5 us
  transfers between devices with their start and end apart: 4, of which 3 were waited for; matrix products, arithmetic and copies ran while one was open for 11% of the time, Pallas kernels for 0%

profile of v1, /device:TPU:33, one launch (start us, length us, event | category | flops | bytes accessed | tf_op | source)
XLA Modules:
  0.0 482.5 jit_solution(7864734396700941871)
XLA Ops:
  7.2 0.0 copy-start
  7.2 0.0 copy-start.2
  7.2 0.0 all-gather.3.cloned.1.call-start
  7.2 6.2 %fusion.13 = (bf16[2,4,384,512]{3,2,1,0:T(8,128)(2,1)}, bf16[2,4,384,512]{3,2,1,0:T(8,128)(2,1)}) fusion(bf16[2,8,384,512]{3,2,1,0:T(8,128)(2,1)} %param.6), kind=kLoop, calls=%fused_computation.20 | loop fusion | bytes 12582912 | tf_op jit(solution)/shard_map/slice | solution.py:14
  13.5 1.8 collective-permute-start
  15.3 0.0 collective-permute-start.1
  15.3 0.1 copy.26
  15.4 0.1 reshape.10
  15.5 0.1 fusion.7
  15.5 34.2 %collective-permute-done = bf16[2,4,384,512]{3,2,1,0:T(8,128)(2,1)} collective-permute-done((bf16[2,4,384,512]{3,2,1,0:T(8,128)(2,1)}, bf16[2,4,384,512]{3,2,1,0:T(8,128)(2,1)}, u32[]{:S(2)}, u32[]{:S(2)}) %collective-permute-start) | collective-permute-done | bytes 3145760 | tf_op jit(solution)/shard_map/ppermute | solution.py:17
  49.8 2.8 collective-permute-done.1
  52.6 10.5 %pad_maximum_fusion = bf16[2,16,384,512]{3,2,1,0:T(8,128)(2,1)} fusion(bf16[2,4,384,512]{3,2,1,0:T(8,128)(2,1)} %collective-permute-done.1, bf16[2,8,384,512]{3,2,1,0:T(8,128)(2,1)} %param.6, bf16[2,4,384,512]{3,2,1,0:T(8,128)(2,1)} %collective-permute-done), kind=kLoop, calls=%fused_computation.1 | loop fusion | flops 12582912 | bytes 25165824 | tf_op jit(solution)/shard_map/concatenate | solution.py:15
  63.1 11.4 %gather_fusion = bf16[32,384,512]{2,1,0:T(8,128)(2,1)} fusion(bf16[2,16,384,512]{3,2,1,0:T(8,128)(2,1)} %pad_maximum_fusion, s32[32]{0:T(128)S(1)} %reshape.10), kind=kCustom, calls=%fused_computation | custom fusion | bytes 25166080 | tf_op jit(solution)/shard_map/vmap()/gather | solution.py:33
  74.5 16.6 %copy.27 = bf16[2,8,2,384,512]{3,4,2,1,0:T(8,128)(2,1)} copy(bf16[2,8,2,384,512]{4,3,2,1,0:T(8,128)(2,1)} %bitcast.25) | data formatting | bytes 25165824 | tf_op jit(solution)/shard_map/vmap()/gather | solution.py:33
  91.1 13.6 %fusion.4 = bf16[8,384,512]{1,2,0:T(8,128)(2,1)} fusion(bf16[2,8,2,384,384]{4,3,2,1,0:T(8,128)(2,1)} %param.7, bf16[2,8,2,384,512]{3,4,2,1,0:T(8,128)(2,1)} %copy.27, bf16[2,8,2]{2,1,0:T(8,128)(2,1)S(1)} %fusion.7), kind=kOutput, calls=%fused_computation.9 | convolution fusion | flops 4839702528 | bytes 25165888 | tf_op jit(solution)/shard_map/lbsij,lbsjr->bir/dot_general | solution.py:44
  104.7 4.7 copy.28
  109.4 0.0 all-gather.3.cloned.1.call-update
  109.5 6.1 %fusion.12 = (bf16[1,8,384,512]{3,2,1,0:T(8,128)(2,1)}, bf16[1,8,384,512]{3,2,1,0:T(8,128)(2,1)}) fusion(bf16[2,8,384,512]{3,2,1,0:T(8,128)(2,1)} %param.6), kind=kLoop, calls=%fused_computation.19 | loop fusion | bytes 12582912 | tf_op jit(solution)/shard_map/slice | solution.py:47
  115.5 4.6 copy.37
  120.2 3.4 collective-permute-start.2
  123.6 6.8 %copy.30 = f32[8,384,512]{1,2,0:T(8,128)} copy(f32[8,384,512]{2,1,0:T(8,128)} %param.9) | data formatting | bytes 12582912 | tf_op args[3]
  130.3 4.7 copy.38
  135.1 293.8 %all-gather.3.cloned.1.call-done = bf16[64,384,512]{2,1,0:T(8,128)(2,1)} async-done(((bf16[8,384,512]{2,1,0:T(8,128)(2,1)}), bf16[64,384,512]{2,1,0:T(8,128)(2,1)}) %all-gather.3.cloned.1.call-update) | async-done | bytes 25165840 | tf_op jit(solution)/shard_map/all_gather | solution.py:48
  428.9 15.3 %reduce_sum.12 = bf16[8,384,512]{2,1,0:T(8,128)(2,1)} reduce(bf16[8,8,384,512]{3,2,1,0:T(8,128)(2,1)} %bitcast.26, bf16[]{:T(256)} %constant.2.clone.1), dimensions={0}, to_apply=%region_0.0 | reduce | flops 11010048 | bytes 28311554 | tf_op jit(solution)/shard_map/reduce_sum | solution.py:48
  444.1 4.6 copy.36
  448.8 7.4 %convert_bitcast_fusion = bf16[8,384,512]{1,2,0:T(8,128)(2,1)} fusion(bf16[8,384,384]{2,1,0:T(8,128)(2,1)S(1)} %copy-done, f32[8,384,512]{1,2,0:T(8,128)} %copy.30, bf16[8,384,512]{1,2,0:T(8,128)(2,1)} %copy.36), kind=kOutput, calls=%fused_computation.11 | convolution fusion | flops 1214251008 | bytes 14942208 | tf_op jit(solution)/shard_map/bij,bjr->bir/dot_general | solution.py:52
  456.2 4.6 copy.33
  460.9 0.0 collective-permute-done.2
  460.9 2.4 select_bitcast_fusion
  463.3 0.4 copy-done.1
  463.7 3.4 pad_maximum_fusion.1
  467.1 8.6 %copy.34 = bf16[2,8,384,512]{3,2,1,0:T(8,128)(2,1)} copy(bf16[2,8,384,512]{2,3,1,0:T(8,128)(2,1)} %pad_maximum_fusion.1) | data formatting | bytes 12582912
  (6 shorter events, 0.0 us)
Async XLA Ops:
  7.2 441.6 %copy-start = (bf16[8,384,384]{2,1,0:T(8,128)(2,1)S(1)}, bf16[8,384,384]{2,1,0:T(8,128)(2,1)}, u32[]{:S(2)}) copy-start(bf16[8,384,384]{2,1,0:T(8,128)(2,1)} %param.8) | copy-start | bytes 7077892
  7.2 8.1 %copy-start.2 = (s32[2,8,2]{1,2,0:T(2,128)S(1)}, s32[2,8,2]{1,2,0:T(2,128)}, u32[]{:S(2)}) copy-start(s32[2,8,2]{1,2,0:T(2,128)} %param.10) | copy-start | bytes 388
  7.2 8.3 %copy-start.3 = (s32[2,8]{1,0:T(2,128)S(1)}, s32[2,8]{1,0:T(2,128)}, u32[]{:S(2)}) copy-start(s32[2,8]{1,0:T(2,128)} %param.11) | copy-start | bytes 196
  7.2 421.7 %all-gather.3.cloned.1.call-start = ((), (), s32[]{:S(2)}) async-start(), calls=%async_computation | async-start | bytes 28311552 | tf_op jit(solution)/shard_map/all_gather | solution.py:48
  13.5 36.3 %collective-permute-start = (bf16[2,4,384,512]{3,2,1,0:T(8,128)(2,1)}, bf16[2,4,384,512]{3,2,1,0:T(8,128)(2,1)}, u32[]{:S(2)}, u32[]{:S(2)}) collective-permute-start(bf16[2,4,384,512]{3,2,1,0:T(8,128)(2,1)} %get-tuple-element.10), channel_id=1, source_target_pairs={{0,8},{8,16},{16,24},{24,32},{32,40},{40,48},{48,56},{56,64},{64,7... | collective-permute-start | bytes 9437192 | tf_op jit(solution)/shard_map/ppermute | solution.py:17
  15.3 37.3 %collective-permute-start.1 = (bf16[2,4,384,512]{3,2,1,0:T(8,128)(2,1)}, bf16[2,4,384,512]{3,2,1,0:T(8,128)(2,1)}, u32[]{:S(2)}, u32[]{:S(2)}) collective-permute-start(bf16[2,4,384,512]{3,2,1,0:T(8,128)(2,1)} %get-tuple-element.11), channel_id=1, source_target_pairs={{8,0},{16,8},{24,16},{32,24},{40,32},{48,40},{56,48},{64,56},{72,6... | collective-permute-start | bytes 9437192 | tf_op jit(solution)/shard_map/ppermute | solution.py:19
  120.2 340.7 %collective-permute-start.2 = (bf16[8,384,512]{1,2,0:T(8,128)(2,1)}, bf16[8,384,512]{1,2,0:T(8,128)(2,1)}, u32[]{:S(2)}, u32[]{:S(2)}) collective-permute-start(bf16[8,384,512]{1,2,0:T(8,128)(2,1)} %bitcast.27), channel_id=1, source_target_pairs={{0,1},{1,2},{2,3},{3,4},{4,5},{5,6},{6,7},{8,9},{9,10},{10,11},{11... | collective-permute-start | bytes 9437192 | tf_op jit(solution)/shard_map/ppermute | solution.py:29
  460.9 2.8 copy-start.1
Sparse Core Ops, SparseCore 0:
  109.6 319.2 all-gather.2
